TPU v7x, 512 devices: a whole 4x4x16 slice. The times are simulated.
512 devices in a mesh: dp: 8 (over x, core), expert: 64 (over y, z).
Axes of the slice: x: 4, y: 4, z: 16, core: 2. Of those that a mesh axis runs over, the one named last changes fastest.
Arguments:
- tokens: bfloat16 [65536, 1024], P(('dp', 'expert')), may hold values from -6 to 6
- grad_out: bfloat16 [65536, 1024], P(('dp', 'expert')), may hold values from -6 to 6
- expert_ids: int32 [65536, 8], P(('dp', 'expert')), may hold values from 0 to 63, all different within a row; in each aligned block of 128 rows (0 to 127, 128 to 255, ...) at most 18 rows name the same one
- gates: float32 [65536, 8], P(('dp', 'expert')), may hold values from 0.1 to 0.5
- w_in: bfloat16 [64, 1024, 768], P('expert', 'dp'), may hold values from -0.1875 to 0.1875
- w_down: bfloat16 [64, 384, 1024], P('expert', 'dp'), may hold values from -0.3125 to 0.3125
Outputs:
- grad_tokens: bfloat16 [65536, 1024], P(('dp', 'expert'))
- grad_in: float32 [64, 1024, 768], P('expert', 'dp')
- grad_down: float32 [64, 384, 1024], P('expert', 'dp')
Inputs may be any that keep to these rules, and one draw needn't show every extreme that they name: `expert_ids`: each token names 8 different experts; among the tokens of one device no expert is named more than 18 times, a bound that some block reaches.
All inputs are finite; a program needn't handle non-finite values.
Results may differ from a plain program's by a relative error of at most 0.015.
Values may be sent and summed in bfloat16 or wider, within the bound.
No kernel may reach another device: no remote copies, remote signals or barrier semaphores. Data moves between devices by JAX's collectives and lax.ppermute only.
A program may use at most 64 MiB of HBM per device.

v0:
```python
import jax
import jax.numpy as jnp
from jax import lax
from jax.sharding import Mesh
from jax.sharding import PartitionSpec as P


def hidden_from(preact):
    half_width = preact.shape[1] // 2
    gate_pre = preact[:, :half_width]
    up_pre = preact[:, half_width:]
    sigmoid_gate = jax.nn.sigmoid(gate_pre)
    return (gate_pre * sigmoid_gate * up_pre).astype(jnp.bfloat16)


def pre_grads(preact, grad_hidden):
    half_width = preact.shape[1] // 2
    gate_pre = preact[:, :half_width]
    up_pre = preact[:, half_width:]
    sigmoid_gate = jax.nn.sigmoid(gate_pre)
    grad_gate = grad_hidden * up_pre * sigmoid_gate * (1.0 + gate_pre * (1.0 - sigmoid_gate))
    grad_up = grad_hidden * gate_pre * sigmoid_gate
    return jnp.concatenate([grad_gate, grad_up], axis=1).astype(jnp.bfloat16)


def contract_first(left, right):
    return lax.dot_general(
        left, right, (((0,), (0,)), ((), ())), preferred_element_type=jnp.float32
    )


def contract_last(left, right):
    return lax.dot_general(
        left, right, (((1,), (1,)), ((), ())), preferred_element_type=jnp.float32
    )


def expert_exchange(blocks, rows, cols):
    capacity, width = (blocks.shape[1], blocks.shape[2])
    blocks = blocks.reshape(rows, cols, capacity, width)
    blocks = lax.all_to_all(blocks, "ez", 1, 1, tiled=True)
    blocks = lax.all_to_all(blocks, "ey", 0, 0, tiled=True)
    return blocks.reshape(rows * cols, capacity, width)


def on_device(tokens, grad_out, expert_ids, gates, w_in, w_down):
    token_rows, model_width = tokens.shape
    route_width = expert_ids.shape[1]
    rows = lax.axis_size("ey")
    cols = lax.axis_size("ez")
    expert_count = rows * cols
    route_total = token_rows * route_width
    capacity = route_total // expert_count + max(1, route_total // (8 * expert_count))
    slot_total = expert_count * capacity
    flat_ids = expert_ids.reshape(route_total)
    route_marks = (flat_ids[:, None] == jnp.arange(expert_count, dtype=jnp.int32)[None, :]).astype(
        jnp.int32
    )
    route_index = jnp.arange(route_total, dtype=jnp.int32)
    lower_table = (route_index[None, :] <= route_index[:, None]).astype(jnp.bfloat16)
    running = jnp.dot(
        lower_table, route_marks.astype(jnp.bfloat16), preferred_element_type=jnp.float32
    )
    slot_ranks = jnp.sum((running.astype(jnp.int32) - 1) * route_marks, axis=1)
    targets = (flat_ids * capacity + slot_ranks).reshape(token_rows, route_width)
    slot_index = jnp.arange(slot_total, dtype=jnp.int32)
    slot_hits = targets[None, :, :] == slot_index[:, None, None]
    slot_of_token = jnp.any(slot_hits, axis=2).astype(jnp.bfloat16)
    slot_gates = jnp.sum(jnp.where(slot_hits, gates[None, :, :], 0.0), axis=(1, 2))
    send_tokens = jnp.dot(slot_of_token, tokens, preferred_element_type=jnp.float32).astype(
        jnp.bfloat16
    )
    picked_grads = jnp.dot(slot_of_token, grad_out, preferred_element_type=jnp.float32)
    send_grads = (slot_gates[:, None] * picked_grads).astype(jnp.bfloat16)
    send_both = jnp.concatenate([send_tokens, send_grads], axis=1)
    recv_both = expert_exchange(
        send_both.reshape(expert_count, capacity, 2 * model_width), rows, cols
    ).reshape(slot_total, 2 * model_width)
    slot_tokens = recv_both[:, :model_width]
    slot_grads = recv_both[:, model_width:]
    local_in = w_in[0]
    local_down = w_down[0]
    full_in, full_down = (
        lax.all_gather(local_in, "dp", axis=0, tiled=True),
        lax.all_gather(local_down, "dp", axis=0, tiled=True),
    )
    preact = jnp.dot(slot_tokens, full_in, preferred_element_type=jnp.float32)
    grad_hidden = contract_last(slot_grads, full_down)
    pre_grad = pre_grads(preact, grad_hidden)
    slot_back = contract_last(pre_grad, full_in).astype(jnp.bfloat16)
    hidden_act = hidden_from(preact)
    grad_in_local = lax.psum_scatter(
        contract_first(slot_tokens, pre_grad).astype(jnp.bfloat16),
        "dp",
        scatter_dimension=0,
        tiled=True,
    ).astype(jnp.float32)
    grad_down_local = lax.psum_scatter(
        contract_first(hidden_act, slot_grads).astype(jnp.bfloat16),
        "dp",
        scatter_dimension=0,
        tiled=True,
    ).astype(jnp.float32)
    slot_return = expert_exchange(
        slot_back.reshape(expert_count, capacity, model_width), rows, cols
    ).reshape(slot_total, model_width)
    grad_tokens = contract_first(slot_of_token, slot_return).astype(jnp.bfloat16)
    return (grad_tokens, grad_in_local[None], grad_down_local[None])


def solution(mesh):
    dp_size = mesh.shape["dp"]
    expert_devices = mesh.devices.reshape(dp_size, -1)
    rows = 4 if expert_devices.shape[1] % 4 == 0 else 1
    split_mesh = Mesh(
        expert_devices.reshape(dp_size, rows, expert_devices.shape[1] // rows), ("dp", "ey", "ez")
    )
    token_spec = P(("dp", "ey", "ez"), None)
    weight_spec = P(("ey", "ez"), "dp", None)
    in_specs = (token_spec, token_spec, token_spec, token_spec, weight_spec, weight_spec)
    out_specs = (token_spec, weight_spec, weight_spec)
    return jax.shard_map(
        on_device, mesh=split_mesh, in_specs=in_specs, out_specs=out_specs, check_vma=False
    )
```

profile of v0, /device:TPU:38, one launch (start us, length us, event | category | flops | bytes accessed | tf_op | source)
XLA Modules:
  0.0 530.4 jit_solution(8605643046941876970)
XLA Ops:
  9.6 4.2 fusion
  13.8 9.3 %select_reduce_fusion = f32[1152]{0:T(1024)S(1)} fusion(f32[128,8]{0,1:T(8,128)} %param.9, s32[128,8]{0,1:T(8,128)S(1)} %multiply_add_fusion), kind=kLoop, calls=%fused_computation.2 | loop fusion | flops 3537792 | bytes 12800 | tf_op jit(solution)/shard_map/reduce_sum | solution.py:69
  27.3 6.8 %copy.40 = bf16[1152,2048]{1,0:T(8,128)(2,1)} copy(bf16[1152,2048]{0,1:T(8,128)(2,1)} %pad_maximum_fusion) | data formatting | bytes 9437184 | tf_op jit(solution)/shard_map/concatenate | solution.py:75
  34.1 7.6 %reshape_reshape.12 = bf16[4,16,18,2048]{3,2,1,0:T(8,128)(2,1)} reshape(bf16[1152,2048]{1,0:T(8,128)(2,1)} %copy.40) | data formatting | bytes 9437184 | tf_op jit(solution)/shard_map/reshape;reshape | solution.py:40
  41.7 6.8 %copy.41 = bf16[4,16,18,2048]{3,0,2,1:T(4,128)(2,1)S(1)} copy(bf16[4,16,18,2048]{3,2,1,0:T(8,128)(2,1)} %reshape_reshape.12) | data formatting | bytes 9437184 | tf_op jit(solution)/shard_map/reshape;reshape | solution.py:40
  48.5 223.2 %all_to_all.20 = bf16[4,16,18,2048]{3,0,2,1:T(4,128)(2,1)S(1)} all-to-all(bf16[4,16,18,2048]{3,0,2,1:T(4,128)(2,1)S(1)} %copy.41), channel_id=1, replica_groups=mesh['dp'=8,'ey'=4,'ez'=16] {'ez'}, dimensions={1} | all-to-all | bytes 9437184 | tf_op jit(solution)/shard_map/all_to_all | solution.py:41
  271.7 4.7 copy.42
  276.4 5.1 all-to-all-start.1
  282.3 13.4 %all-gather = bf16[1,384,1024]{2,1,0:T(8,128)(2,1)S(1)} all-gather(bf16[1,48,1024]{2,1,0:T(8,128)(2,1)S(1)} %copy-done.4), channel_id=2, replica_groups=mesh['dp'=8,'ey'=4,'ez'=16] {'dp'}, dimensions={1}, use_global_device_ids=true | all-gather | bytes 884736 | tf_op jit(solution)/shard_map/all_gather | solution.py:85
  295.6 36.4 %all-to-all-done.1 = bf16[4,16,18,2048]{3,1,2,0:T(8,128)(2,1)} async-done(((bf16[4,16,18,2048]{3,1,2,0:T(8,128)(2,1)}), bf16[4,16,18,2048]{3,1,2,0:T(8,128)(2,1)}, u32[]{:S(2)}, u32[]{:S(2)}) %all-to-all-start.1) | async-done | bytes 4718624 | tf_op jit(solution)/shard_map/all_to_all | solution.py:42
  332.1 7.9 %copy.43 = bf16[4,16,18,2048]{3,2,1,0:T(8,128)(2,1)} copy(bf16[4,16,18,2048]{3,1,2,0:T(8,128)(2,1)} %all-to-all-done.1) | data formatting | bytes 9437184 | tf_op jit(solution)/shard_map/all_to_all | solution.py:42
  340.0 7.7 %reshape_reshape.13 = bf16[1152,2048]{1,0:T(8,128)(2,1)} reshape(bf16[4,16,18,2048]{3,2,1,0:T(8,128)(2,1)} %copy.43) | data formatting | bytes 9437184 | tf_op jit(solution)/shard_map/reshape;reshape | solution.py:78
  347.8 4.6 fusion.5
  355.5 3.5 convolution_convert_fusion
  361.8 3.4 copy.44
  365.2 11.2 %all-to-all-start.2 = ((bf16[4,16,18,1024]{3,0,2,1:T(4,128)(2,1)}), bf16[4,16,18,1024]{3,0,2,1:T(4,128)(2,1)S(1)}, u32[]{:S(2)}, u32[]{:S(2)}) async-start(bf16[4,16,18,1024]{3,0,2,1:T(4,128)(2,1)} %copy.44), calls=%async_computation.2 | async-start | bytes 4718592 | tf_op jit(solution)/shard_map/all_to_all | solution.py:41
  376.4 4.9 fusion.16
  381.6 5.6 %fusion.11 = bf16[1024,768]{1,0:T(8,128)(2,1)} fusion(bf16[1152,2048]{1,0:T(8,128)(2,1)} %reshape_reshape.13, bf16[1152,384]{0,1:T(8,128)(2,1)} %copy-done.8, bf16[1152,384]{0,1:T(8,128)(2,1)} %copy-done.7), kind=kOutput, calls=%fused_computation.23 | convolution fusion | flops 1816264704 | bytes 5701632 | tf_op jit(solution)/shard_map/dot_general | solution.py:27
  387.2 92.5 %all-to-all-done.2 = bf16[4,16,18,1024]{3,0,2,1:T(4,128)(2,1)S(1)} async-done(((bf16[4,16,18,1024]{3,0,2,1:T(4,128)(2,1)}), bf16[4,16,18,1024]{3,0,2,1:T(4,128)(2,1)S(1)}, u32[]{:S(2)}, u32[]{:S(2)}) %all-to-all-start.2) | async-done | bytes 2359328 | tf_op jit(solution)/shard_map/all_to_all | solution.py:41
  479.7 2.7 copy.45
  482.5 4.5 all-to-all-start.3
  490.3 25.3 %all-to-all-done.3 = bf16[4,16,18,1024]{3,1,2,0:T(8,128)(2,1)} async-done(((bf16[4,16,18,1024]{3,1,2,0:T(8,128)(2,1)}), bf16[4,16,18,1024]{3,1,2,0:T(8,128)(2,1)}, u32[]{:S(2)}, u32[]{:S(2)}) %all-to-all-start.3) | async-done | bytes 2359328 | tf_op jit(solution)/shard_map/all_to_all | solution.py:42
  515.6 3.1 copy.46
  520.9 2.9 convolution_convert_fusion.2
  (41 shorter events, 19.0 us)
Async XLA Ops:
  7.2 15.9 %copy-start = (bf16[128,1024]{1,0:T(8,128)(2,1)S(1)}, bf16[128,1024]{1,0:T(8,128)(2,1)}, u32[]{:S(2)}) copy-start(bf16[128,1024]{1,0:T(8,128)(2,1)} %param.6) | copy-start | bytes 786436
  8.1 15.8 %copy-start.3 = (bf16[128,1024]{1,0:T(8,128)(2,1)S(1)}, bf16[128,1024]{1,0:T(8,128)(2,1)}, u32[]{:S(2)}) copy-start(bf16[128,1024]{1,0:T(8,128)(2,1)} %param.7) | copy-start | bytes 786436
  276.4 5.8 %copy-start.4 = (bf16[1,48,1024]{2,1,0:T(8,128)(2,1)S(1)}, bf16[1,48,1024]{2,1,0:T(8,128)(2,1)}, u32[]{:S(2)}) copy-start(bf16[1,48,1024]{2,1,0:T(8,128)(2,1)} %param.11) | copy-start | bytes 294916
  276.4 55.7 %all-to-all-start.1 = ((bf16[4,16,18,2048]{3,1,2,0:T(8,128)(2,1)}), bf16[4,16,18,2048]{3,1,2,0:T(8,128)(2,1)}, u32[]{:S(2)}, u32[]{:S(2)}) async-start(bf16[4,16,18,2048]{3,1,2,0:T(8,128)(2,1)} %copy.42), calls=%async_computation.1 | async-start | bytes 9437184 | tf_op jit(solution)/shard_map/all_to_all | solution.py:42
  281.5 66.2 %all-gather.4.cloned.1.call-start = ((), (), s32[]{:S(2)}) async-start(), calls=%async_computation.8 | async-start | bytes 1769472 | tf_op jit(solution)/shard_map/all_gather | solution.py:84
  347.8 4.7 copy-start.2
  352.4 1.9 copy-start.6
  352.4 3.1 copy-start.5
  354.3 0.9 copy-start.7
  354.3 1.2 copy-start.8
  365.2 114.5 %all-to-all-start.2 = ((bf16[4,16,18,1024]{3,0,2,1:T(4,128)(2,1)}), bf16[4,16,18,1024]{3,0,2,1:T(4,128)(2,1)S(1)}, u32[]{:S(2)}, u32[]{:S(2)}) async-start(bf16[4,16,18,1024]{3,0,2,1:T(4,128)(2,1)} %copy.44), calls=%async_computation.2 | async-start | bytes 4718592 | tf_op jit(solution)/shard_map/all_to_all | solution.py:41
  376.4 110.6 %reduce-scatter.5.cloned.1.call-start = ((), (), s32[]{:S(2)}) async-start(), calls=%async_computation.7 | async-start | bytes 884736 | tf_op jit(solution)/shard_map/reduce_scatter | solution.py:98
  381.3 107.3 %reduce-scatter.3.cloned.1.call-start = ((), (), s32[]{:S(2)}) async-start(), calls=%async_computation.6 | async-start | bytes 1769472 | tf_op jit(solution)/shard_map/reduce_scatter | solution.py:92
  482.5 33.1 %all-to-all-start.3 = ((bf16[4,16,18,1024]{3,1,2,0:T(8,128)(2,1)}), bf16[4,16,18,1024]{3,1,2,0:T(8,128)(2,1)}, u32[]{:S(2)}, u32[]{:S(2)}) async-start(bf16[4,16,18,1024]{3,1,2,0:T(8,128)(2,1)} %copy.45), calls=%async_computation.3 | async-start | bytes 4718592 | tf_op jit(solution)/shard_map/all_to_all | solution.py:42
  518.7 5.2 copy-start.1
Sparse Core Ops, SparseCore 0:
  284.4 26.4 all-gather.3
  381.4 35.7 reduce-scatter.4
  420.1 40.1 reduce-scatter.2
where the time goes:
time: 532 us; the launch traced here: 530 us
  blocking collectives  237 us (45%)
  waiting for transfers between devices  155 us (29%)
  local copies, waits for them, and re-layouts  58.2 us (11%)
  matrix products  25.5 us (5%)
  starting transfers between devices  21.1 us (4%)
  other arithmetic  20.1 us (4%)
  between operations  13.9 us (3%)
    all_to_all x1, blocking collectives, expert_exchange(): blocks = lax.all_to_all(blocks, 'ez', 1, 1, tiled=True)  223 us
    all_to_all x1, waiting for transfers between devices, expert_exchange(): blocks = lax.all_to_all(blocks, 'ez', 1, 1, tiled=True)  92.5 us
    all_to_all x2, waiting for transfers between devices, expert_exchange(): blocks = lax.all_to_all(blocks, 'ey', 0, 0, tiled=True)  61.8 us
    another operation x4, local copies, waits for them, and re-layouts, expert_exchange(): blocks = blocks.reshape(rows, cols, capacity, width)  20.5 us
    dot_general x3, matrix products, contract_first(): lax.dot_general(left, right, (((0,), (0,)), ((), ())), preferred_element_...  13.4 us
    all_gather x1, blocking collectives, on_device(): lax.all_gather(local_down, 'dp', axis=0, tiled=True)  13.4 us
    all_to_all x1, starting transfers between devices, expert_exchange(): blocks = lax.all_to_all(blocks, 'ez', 1, 1, tiled=True)  11.2 us
    all_to_all x2, local copies, waits for them, and re-layouts, expert_exchange(): blocks = lax.all_to_all(blocks, 'ey', 0, 0, tiled=True)  11 us
  transfers between devices with their start and end apart: 6, of which 3 were waited for; matrix products, arithmetic and copies ran while one was open for 6% of the time, Pallas kernels for 0%

commit v1 on v0

--- a/solution.py
+++ b/solution.py
@@ -82,7 +82,15 @@
     local_down = w_down[0]
     full_in, full_down = (
         lax.all_gather(local_in, "dp", axis=0, tiled=True),
-        lax.all_gather(local_down, "dp", axis=0, tiled=True),
+        jnp.concatenate(
+            lax.all_to_all(
+                jnp.stack([local_down] * lax.axis_size("dp")),
+                axis_name="dp",
+                split_axis=0,
+                concat_axis=0,
+            ),
+            axis=0,
+        ),
     )
     preact = jnp.dot(slot_tokens, full_in, preferred_element_type=jnp.float32)
     grad_hidden = contract_last(slot_grads, full_down)

time: 532 us -> 543 us (1.021)
  the two profiles are of different devices: /device:TPU:38 before, /device:TPU:32 now
where the time goes in v1:
time: 543 us; the launch traced here: 542 us
  blocking collectives  223 us (41%)
  waiting for transfers between devices  170 us (31%)
  local copies, waits for them, and re-layouts  59.2 us (11%)
  matrix products  29.9 us (6%)
  starting transfers between devices  25.4 us (5%)
  other arithmetic  20.1 us (4%)
  between operations  13.9 us (3%)
    all_to_all x1, blocking collectives, expert_exchange(): blocks = lax.all_to_all(blocks, 'ez', 1, 1, tiled=True)  223 us
    all_to_all x1, waiting for transfers between devices, expert_exchange(): blocks = lax.all_to_all(blocks, 'ez', 1, 1, tiled=True)  94 us
    all_to_all x2, waiting for transfers between devices, expert_exchange(): blocks = lax.all_to_all(blocks, 'ey', 0, 0, tiled=True)  75.5 us
    another operation x4, local copies, waits for them, and re-layouts, expert_exchange(): blocks = blocks.reshape(rows, cols, capacity, width)  20.6 us
    dot_general x3, matrix products, contract_first(): lax.dot_general(left, right, (((0,), (0,)), ((), ())), preferred_element_...  13.4 us
    all_to_all x1, starting transfers between devices, expert_exchange(): blocks = lax.all_to_all(blocks, 'ez', 1, 1, tiled=True)  11.2 us
    all_to_all x2, local copies, waits for them, and re-layouts, expert_exchange(): blocks = lax.all_to_all(blocks, 'ey', 0, 0, tiled=True)  11 us
  transfers between devices with their start and end apart: 7, of which 3 were waited for; matrix products, arithmetic and copies ran while one was open for 7% of the time, Pallas kernels for 0%

profile of v1, /device:TPU:32, one launch (start us, length us, event | category | flops | bytes accessed | tf_op | source)
XLA Modules:
  0.0 541.9 jit_solution(4121309988977753090)
XLA Ops:
  9.6 4.2 fusion
  13.8 9.3 %select_reduce_fusion = f32[1152]{0:T(1024)S(1)} fusion(f32[128,8]{0,1:T(8,128)} %param.9, s32[128,8]{0,1:T(8,128)S(1)} %multiply_add_fusion), kind=kLoop, calls=%fused_computation.2 | loop fusion | flops 3537792 | bytes 12800 | tf_op jit(solution)/shard_map/reduce_sum | solution.py:69
  27.3 6.8 %copy.40 = bf16[1152,2048]{1,0:T(8,128)(2,1)} copy(bf16[1152,2048]{0,1:T(8,128)(2,1)} %pad_maximum_fusion) | data formatting | bytes 9437184 | tf_op jit(solution)/shard_map/concatenate | solution.py:75
  34.1 7.6 %reshape_reshape.12 = bf16[4,16,18,2048]{3,2,1,0:T(8,128)(2,1)} reshape(bf16[1152,2048]{1,0:T(8,128)(2,1)} %copy.40) | data formatting | bytes 9437184 | tf_op jit(solution)/shard_map/reshape;reshape | solution.py:40
  41.7 6.8 %copy.41 = bf16[4,16,18,2048]{3,0,2,1:T(4,128)(2,1)S(1)} copy(bf16[4,16,18,2048]{3,2,1,0:T(8,128)(2,1)} %reshape_reshape.12) | data formatting | bytes 9437184 | tf_op jit(solution)/shard_map/reshape;reshape | solution.py:40
  48.5 223.2 %all_to_all.25 = bf16[4,16,18,2048]{3,0,2,1:T(4,128)(2,1)S(1)} all-to-all(bf16[4,16,18,2048]{3,0,2,1:T(4,128)(2,1)S(1)} %copy.41), channel_id=1, replica_groups=mesh['dp'=8,'ey'=4,'ez'=16] {'ez'}, dimensions={1} | all-to-all | bytes 9437184 | tf_op jit(solution)/shard_map/all_to_all | solution.py:41
  271.7 4.8 copy.42
  276.5 5.1 all-to-all-start.1
  282.4 49.8 %all-to-all-done.1 = bf16[4,16,18,2048]{3,1,2,0:T(8,128)(2,1)} async-done(((bf16[4,16,18,2048]{3,1,2,0:T(8,128)(2,1)}), bf16[4,16,18,2048]{3,1,2,0:T(8,128)(2,1)}, u32[]{:S(2)}, u32[]{:S(2)}) %all-to-all-start.1) | async-done | bytes 4718624 | tf_op jit(solution)/shard_map/all_to_all | solution.py:42
  333.2 4.3 all-to-all-start.2
  337.5 7.9 %copy.43 = bf16[4,16,18,2048]{3,2,1,0:T(8,128)(2,1)} copy(bf16[4,16,18,2048]{3,1,2,0:T(8,128)(2,1)} %all-to-all-done.1) | data formatting | bytes 9437184 | tf_op jit(solution)/shard_map/all_to_all | solution.py:42
  345.4 7.7 %reshape_reshape.13 = bf16[1152,2048]{1,0:T(8,128)(2,1)} reshape(bf16[4,16,18,2048]{3,2,1,0:T(8,128)(2,1)} %copy.43) | data formatting | bytes 9437184 | tf_op jit(solution)/shard_map/reshape;reshape | solution.py:78
  353.1 6.2 %fusion.5 = f32[1152,768]{0,1:T(8,128)} fusion(bf16[1152,2048]{1,0:T(8,128)(2,1)} %reshape_reshape.13, bf16[1,1024,768]{2,1,0:T(8,128)(2,1)} %all-gather.3.cloned.1.call-done), kind=kOutput, calls=%fused_computation.12 | convolution fusion | flops 1811939328 | bytes 7471104 | tf_op jit(solution)/shard_map/dot_general | solution.py:95
  359.4 4.4 multiply_convert_fusion.2
  365.0 3.6 convolution_convert_fusion
  371.3 3.5 copy.44
  374.8 11.2 %all-to-all-start.3 = ((bf16[4,16,18,1024]{3,0,2,1:T(4,128)(2,1)}), bf16[4,16,18,1024]{3,0,2,1:T(4,128)(2,1)S(1)}, u32[]{:S(2)}, u32[]{:S(2)}) async-start(bf16[4,16,18,1024]{3,0,2,1:T(4,128)(2,1)} %copy.44), calls=%async_computation.3 | async-start | bytes 4718592 | tf_op jit(solution)/shard_map/all_to_all | solution.py:41
  386.3 4.9 fusion.16
  391.2 5.6 %fusion.11 = bf16[1024,768]{1,0:T(8,128)(2,1)} fusion(bf16[1152,2048]{1,0:T(8,128)(2,1)} %reshape_reshape.13, bf16[1152,384]{0,1:T(8,128)(2,1)} %copy-done.6, bf16[1152,384]{0,1:T(8,128)(2,1)} %copy-done.5), kind=kOutput, calls=%fused_computation.23 | convolution fusion | flops 1816264704 | bytes 5701632 | tf_op jit(solution)/shard_map/dot_general | solution.py:27
  396.9 94.0 %all-to-all-done.3 = bf16[4,16,18,1024]{3,0,2,1:T(4,128)(2,1)S(1)} async-done(((bf16[4,16,18,1024]{3,0,2,1:T(4,128)(2,1)}), bf16[4,16,18,1024]{3,0,2,1:T(4,128)(2,1)S(1)}, u32[]{:S(2)}, u32[]{:S(2)}) %all-to-all-start.3) | async-done | bytes 2359328 | tf_op jit(solution)/shard_map/all_to_all | solution.py:41
  493.6 4.5 all-to-all-start.4
  501.4 25.7 %all-to-all-done.4 = bf16[4,16,18,1024]{3,1,2,0:T(8,128)(2,1)} async-done(((bf16[4,16,18,1024]{3,1,2,0:T(8,128)(2,1)}), bf16[4,16,18,1024]{3,1,2,0:T(8,128)(2,1)}, u32[]{:S(2)}, u32[]{:S(2)}) %all-to-all-start.4) | async-done | bytes 2359328 | tf_op jit(solution)/shard_map/all_to_all | solution.py:42
  527.1 3.1 copy.46
  532.4 2.9 convolution_convert_fusion.2
  (39 shorter events, 20.9 us)
Async XLA Ops:
  7.2 15.9 %copy-start = (bf16[128,1024]{1,0:T(8,128)(2,1)S(1)}, bf16[128,1024]{1,0:T(8,128)(2,1)}, u32[]{:S(2)}) copy-start(bf16[128,1024]{1,0:T(8,128)(2,1)} %param.6) | copy-start | bytes 786436
  8.1 15.8 %copy-start.2 = (bf16[128,1024]{1,0:T(8,128)(2,1)S(1)}, bf16[128,1024]{1,0:T(8,128)(2,1)}, u32[]{:S(2)}) copy-start(bf16[128,1024]{1,0:T(8,128)(2,1)} %param.7) | copy-start | bytes 786436
  276.5 55.7 %copy-start.3 = (bf16[1,48,1024]{2,1,0:T(8,128)(2,1)S(1)}, bf16[1,48,1024]{2,1,0:T(8,128)(2,1)}, u32[]{:S(2)}) copy-start(bf16[1,48,1024]{2,1,0:T(8,128)(2,1)} %param.11) | copy-start | bytes 294916
  276.5 55.7 %all-to-all-start.1 = ((bf16[4,16,18,2048]{3,1,2,0:T(8,128)(2,1)}), bf16[4,16,18,2048]{3,1,2,0:T(8,128)(2,1)}, u32[]{:S(2)}, u32[]{:S(2)}) async-start(bf16[4,16,18,2048]{3,1,2,0:T(8,128)(2,1)} %copy.42), calls=%async_computation.1 | async-start | bytes 9437184 | tf_op jit(solution)/shard_map/all_to_all | solution.py:42
  281.6 71.5 %all-gather.3.cloned.1.call-start = ((), (), s32[]{:S(2)}) async-start(), calls=%async_computation.9 | async-start | bytes 1769472 | tf_op jit(solution)/shard_map/all_gather | solution.py:84
  333.2 26.2 %all-to-all-start.2 = ((bf16[8,48,1024]{2,1,0:T(8,128)(2,1)}), bf16[8,48,1024]{2,1,0:T(8,128)(2,1)S(1)}, u32[]{:S(2)}, u32[]{:S(2)}) async-start(bf16[8,48,1024]{2,1,0:T(8,128)(2,1)} %stack.3), calls=%async_computation.2 | async-start | bytes 1572864 | tf_op jit(solution)/shard_map/all_to_all | solution.py:86
  359.4 5.6 %copy-start.4 = (bf16[1,1024,768]{2,1,0:T(8,128)(2,1)S(1)}, bf16[1,1024,768]{2,1,0:T(8,128)(2,1)}, u32[]{:S(2)}) copy-start(bf16[1,1024,768]{2,1,0:T(8,128)(2,1)} %all-gather.3.cloned.1.call-done) | copy-start | bytes 4718596
  363.8 0.9 copy-start.5
  363.8 1.2 copy-start.6
  374.8 116.1 %all-to-all-start.3 = ((bf16[4,16,18,1024]{3,0,2,1:T(4,128)(2,1)}), bf16[4,16,18,1024]{3,0,2,1:T(4,128)(2,1)S(1)}, u32[]{:S(2)}, u32[]{:S(2)}) async-start(bf16[4,16,18,1024]{3,0,2,1:T(4,128)(2,1)} %copy.44), calls=%async_computation.3 | async-start | bytes 4718592 | tf_op jit(solution)/shard_map/all_to_all | solution.py:41
  386.0 112.2 %reduce-scatter.5.cloned.1.call-start = ((), (), s32[]{:S(2)}) async-start(), calls=%async_computation.8 | async-start | bytes 884736 | tf_op jit(solution)/shard_map/reduce_scatter | solution.py:106
  391.2 108.5 %reduce-scatter.3.cloned.1.call-start = ((), (), s32[]{:S(2)}) async-start(), calls=%async_computation.7 | async-start | bytes 1769472 | tf_op jit(solution)/shard_map/reduce_scatter | solution.py:100
  493.6 33.5 %all-to-all-start.4 = ((bf16[4,16,18,1024]{3,1,2,0:T(8,128)(2,1)}), bf16[4,16,18,1024]{3,1,2,0:T(8,128)(2,1)}, u32[]{:S(2)}, u32[]{:S(2)}) async-start(bf16[4,16,18,1024]{3,1,2,0:T(8,128)(2,1)} %copy.45), calls=%async_computation.4 | async-start | bytes 4718592 | tf_op jit(solution)/shard_map/all_to_all | solution.py:42
  530.2 5.2 copy-start.1
Sparse Core Ops, SparseCore 0:
  284.5 28.0 all-gather.2
  391.3 39.2 reduce-scatter.4
  433.4 40.3 reduce-scatter.2
